TPU v7x, 512 devices: a whole 4x4x16 slice. The times are simulated.
512 devices in a mesh: dp: 16 (over z), expert: 32 (over x, y, core).
Axes of the slice: x: 4, y: 4, z: 16, core: 2. Of those that a mesh axis runs over, the one named last changes fastest.
Arguments:
- x_tokens: bfloat16 [65536, 2048], P(('dp', 'expert')), may hold values from -6 to 6
- grad_out: bfloat16 [65536, 2048], P(('dp', 'expert')), may hold values from -6 to 6
- expert_ids: int32 [65536, 2], P(('dp', 'expert')), may hold values from 0 to 31, all different within a row; in each aligned block of 128 rows (0 to 127, 128 to 255, ...) at most 10 rows name the same one
- route_probs: float32 [65536, 2], P(('dp', 'expert')), may hold values from 0.1 to 1
- w_gate: bfloat16 [32, 2048, 768], P('expert', 'dp'), may hold values from -0.125 to 0.125
- w_up: bfloat16 [32, 2048, 768], P('expert', 'dp'), may hold values from -0.125 to 0.125
- w_down: bfloat16 [32, 2048, 768], P('expert', 'dp'), may hold values from -0.21875 to 0.21875
Outputs:
- grad_x: bfloat16 [65536, 2048], P(('dp', 'expert'))
- grad_probs: bfloat16 [65536, 2], P(('dp', 'expert'))
- grad_w_down: bfloat16 [32, 2048, 768], P('expert', 'dp')
Inputs may be any that keep to these rules, and one draw needn't show every extreme that they name: `expert_ids`: each token names 2 different experts; among the 128 tokens of one device no expert is named by more than 10 routes, and in every draw some device names some expert exactly 10 times.
All inputs are finite; a program needn't handle non-finite values.
Results may differ from a plain program's by a relative error of at most 0.017.
Values may be sent and summed in bfloat16 or wider, within the bound.
No kernel may reach another device: no remote copies, remote signals or barrier semaphores. Data moves between devices by JAX's collectives and lax.ppermute only.
A program may use at most 64 MiB of HBM per device.

v0:
```python
import jax
import jax.numpy as jnp
from jax import lax
from jax.sharding import PartitionSpec as P


def per_device(x_tokens, grad_out, expert_ids, route_probs, w_gate, w_up, w_down):
    tok_count, model_width = x_tokens.shape
    top_count = expert_ids.shape[1]
    n_expert = lax.axis_size("expert")
    capacity = tok_count * top_count * 5 // (4 * n_expert)
    slot_count = n_expert * capacity
    routes = tok_count * top_count
    flat_ids = expert_ids.reshape(routes)
    onehot = (flat_ids[:, None] == jnp.arange(n_expert, dtype=jnp.int32)).astype(jnp.int32)
    route_rank = jnp.sum((jnp.cumsum(onehot, axis=0) - onehot) * onehot, axis=1)
    target = flat_ids * capacity + route_rank
    source = (
        jnp.full((slot_count,), routes, jnp.int32)
        .at[target]
        .set(jnp.arange(routes, dtype=jnp.int32))
    )
    token_of = jnp.where(source < routes, source // top_count, tok_count)
    x_padded = jnp.concatenate([x_tokens, jnp.zeros((1, model_width), jnp.bfloat16)], axis=0)
    dy_padded = jnp.concatenate([grad_out, jnp.zeros((1, model_width), jnp.bfloat16)], axis=0)
    p_padded = jnp.concatenate([route_probs.reshape(routes), jnp.zeros((1,), jnp.float32)]).astype(
        jnp.bfloat16
    )
    x_slots = x_padded[token_of].reshape(n_expert, capacity, model_width)
    dy_slots = dy_padded[token_of].reshape(n_expert, capacity, model_width)
    p_slots = p_padded[source].reshape(n_expert, capacity)
    arrived = (
        lax.all_to_all(x_slots, "expert", split_axis=0, concat_axis=0, tiled=True),
        lax.all_to_all(dy_slots, "expert", split_axis=0, concat_axis=0, tiled=True),
        lax.all_to_all(p_slots, "expert", split_axis=0, concat_axis=0, tiled=True),
    )
    in_rows = arrived[0].reshape(slot_count, model_width)
    dy_rows = arrived[1].reshape(slot_count, model_width)
    p_rows = arrived[2].reshape(slot_count).astype(jnp.float32)
    scaled = (p_rows[:, None] * dy_rows.astype(jnp.float32)).astype(jnp.bfloat16)
    gate_full, up_full = (
        lax.all_gather(w_gate, "dp", axis=1, tiled=True),
        lax.all_gather(w_up, "dp", axis=1, tiled=True),
    )
    gate_full = gate_full[0]
    up_full = up_full[0]
    gate_pre = jnp.dot(in_rows, gate_full, preferred_element_type=jnp.float32)
    up_pre = jnp.dot(in_rows, up_full, preferred_element_type=jnp.float32)
    gate_sig = jax.nn.sigmoid(gate_pre)
    gate_act = gate_pre * gate_sig
    hidden = (gate_act * up_pre).astype(jnp.bfloat16)
    piece_rows = lax.all_gather(w_down, "dp", axis=1, tiled=True)[0]
    out_piece = jnp.dot(hidden, piece_rows.T, preferred_element_type=jnp.float32)
    grad_sum = jnp.dot(scaled, piece_rows, preferred_element_type=jnp.float32)
    prob_sum = jnp.sum(dy_rows.astype(jnp.float32) * out_piece, axis=1)
    hidden_grad, prob_sum = (grad_sum, prob_sum)
    up_grad = (hidden_grad * gate_act).astype(jnp.bfloat16)
    gate_grad = (hidden_grad * up_pre * gate_sig * (1.0 + gate_pre * (1.0 - gate_sig))).astype(
        jnp.bfloat16
    )
    x_grad = (
        jnp.dot(gate_grad, gate_full.T, preferred_element_type=jnp.float32)
        + jnp.dot(up_grad, up_full.T, preferred_element_type=jnp.float32)
    ).astype(jnp.bfloat16)
    down_grad = lax.psum_scatter(
        lax.dot_general(
            scaled, hidden, (((0,), (0,)), ((), ())), preferred_element_type=jnp.float32
        ).astype(jnp.bfloat16),
        "dp",
        scatter_dimension=0,
        tiled=True,
    )
    grad_w_down = down_grad[None]
    returned = (
        lax.all_to_all(
            x_grad.reshape(n_expert, capacity, model_width),
            "expert",
            split_axis=0,
            concat_axis=0,
            tiled=True,
        ),
        lax.all_to_all(
            prob_sum.astype(jnp.bfloat16).reshape(n_expert, capacity),
            "expert",
            split_axis=0,
            concat_axis=0,
            tiled=True,
        ),
    )
    grad_slots = returned[0].reshape(slot_count, model_width)
    prob_slots = returned[1].reshape(slot_count)
    picked = grad_slots[target].astype(jnp.float32).reshape(tok_count, top_count, model_width)
    grad_x = jnp.sum(picked, axis=1).astype(jnp.bfloat16)
    grad_probs = prob_slots[target].reshape(tok_count, top_count)
    return (grad_x, grad_probs, grad_w_down)


def solution(mesh):
    return jax.shard_map(
        per_device,
        mesh=mesh,
        in_specs=(
            P(("dp", "expert"), None),
            P(("dp", "expert"), None),
            P(("dp", "expert"), None),
            P(("dp", "expert"), None),
            P("expert", "dp", None),
            P("expert", "dp", None),
            P("expert", "dp", None),
        ),
        out_specs=(P(("dp", "expert"), None), P(("dp", "expert"), None), P("expert", "dp", None)),
        check_vma=False,
    )
```

profile of v0, /device:TPU:4, one launch (start us, length us, event | category | flops | bytes accessed | tf_op | source)
XLA Modules:
  0.0 322.4 jit_solution(13100136976467206266)
XLA Ops:
  7.2 0.7 all-gather.8.cloned.1.call-update
  8.0 0.7 all-gather.6.cloned.1.call-update
  8.7 0.7 all-gather.4.cloned.1.call-update
  9.4 0.8 copy.18
  10.5 0.7 convert.9
  11.4 0.7 broadcast_multiply_fusion
  12.4 0.6 reduce-window.6
  13.0 0.2 slice_reduce_fusion
  13.3 1.4 scatter_custom_fusion
  14.8 2.5 gather_fusion
  17.3 0.7 all_to_all.25
  18.0 9.4 %all-to-all-start = ((bf16[32,1,10]{2,1,0:T(2,128)(2,1)}), bf16[32,1,10]{2,1,0:T(2,128)(2,1)S(1)}, u32[]{:S(2)}, u32[]{:S(2)}) async-start(bf16[32,1,10]{2,1,0:T(2,128)(2,1)} %all_to_all.25), calls=%async_computation | async-start | bytes 32768 | tf_op jit(solution)/shard_map/all_to_all | solution.py:35
  27.5 2.4 gather_fusion.2
  29.9 1.7 reshape.123
  31.6 1.1 all-to-all-done
  32.7 6.4 %all-to-all-start.2 = ((bf16[32,10,2048]{2,1,0:T(8,128)(2,1)}), bf16[32,10,2048]{2,1,0:T(8,128)(2,1)S(1)}, u32[]{:S(2)}, u32[]{:S(2)}) async-start(bf16[32,10,2048]{2,1,0:T(8,128)(2,1)} %reshape.123), calls=%async_computation.2 | async-start | bytes 4194304 | tf_op jit(solution)/shard_map/all_to_all | solution.py:33
  39.2 3.0 gather_fusion.1
  42.2 3.3 %reshape.122 = bf16[32,10,2048]{2,1,0:T(8,128)(2,1)} reshape(bf16[320,2048]{1,0:T(8,128)(2,1)} %gather_fusion.1) | data formatting | bytes 2621440 | tf_op jit(solution)/shard_map/reshape | solution.py:30
  45.6 19.5 %all-to-all-done.2 = bf16[32,10,2048]{2,1,0:T(8,128)(2,1)S(1)} async-done(((bf16[32,10,2048]{2,1,0:T(8,128)(2,1)}), bf16[32,10,2048]{2,1,0:T(8,128)(2,1)S(1)}, u32[]{:S(2)}, u32[]{:S(2)}) %all-to-all-start.2) | async-done | bytes 1310752 | tf_op jit(solution)/shard_map/all_to_all | solution.py:33
  65.0 7.7 %all-to-all-start.1 = ((bf16[32,10,2048]{2,1,0:T(8,128)(2,1)}), bf16[32,10,2048]{2,1,0:T(8,128)(2,1)}, u32[]{:S(2)}, u32[]{:S(2)}) async-start(bf16[32,10,2048]{2,1,0:T(8,128)(2,1)} %reshape.122), calls=%async_computation.1 | async-start | bytes 4194304 | tf_op jit(solution)/shard_map/all_to_all | solution.py:34
  72.7 0.2 reduce-scatter.2.cloned.1.call-start
  73.1 1.4 reshape.124
  74.5 24.1 %all-to-all-done.1 = bf16[32,10,2048]{2,1,0:T(8,128)(2,1)} async-done(((bf16[32,10,2048]{2,1,0:T(8,128)(2,1)}), bf16[32,10,2048]{2,1,0:T(8,128)(2,1)}, u32[]{:S(2)}, u32[]{:S(2)}) %all-to-all-start.1) | async-done | bytes 1310752 | tf_op jit(solution)/shard_map/all_to_all | solution.py:34
  98.6 2.5 reshape.130
  101.1 4.4 %fusion.2 = f32[320,768]{1,0:T(8,128)} fusion(bf16[320,2048]{1,0:T(8,128)(2,1)} %reshape.124, bf16[1,2048,768]{2,1,0:T(8,128)(2,1)} %all-gather.8.cloned.1.call-done), kind=kOutput, calls=%fused_computation.10 | convolution fusion | flops 1006632960 | bytes 5439488 | tf_op jit(solution)/shard_map/dot_general | solution.py:47
  105.6 58.7 %all-gather.6.cloned.1.call-done = bf16[1,2048,768]{2,1,0:T(8,128)(2,1)} async-done(((bf16[1,128,768]{2,1,0:T(8,128)(2,1)}), bf16[1,2048,768]{2,1,0:T(8,128)(2,1)}) %all-gather.6.cloned.1.call-update) | async-done | bytes 3145744 | tf_op jit(solution)/shard_map/all_gather | solution.py:43
  164.3 4.7 %multiply_convert_fusion.3 = (bf16[320,768]{1,0:T(8,128)(2,1)S(1)}, f32[320,768]{1,0:T(8,128)}) fusion(f32[320,768]{1,0:T(8,128)} %fusion.2, bf16[320,2048]{1,0:T(8,128)(2,1)} %reshape.124, bf16[1,2048,768]{2,1,0:T(8,128)(2,1)} %all-gather.6.cloned.1.call-done), kind=kOutput, calls=%fused_computation.26 | convolution fusion | flops 1008107520 | bytes 6914048 | tf_op jit(solution)/shard_map/dot_general | solution.py:48
  169.0 3.6 %convolution_convert_fusion = bf16[2048,768]{1,0:T(8,128)(2,1)} fusion(bf16[320,768]{1,0:T(8,128)(2,1)S(1)} %get-tuple-element.11, f32[320,2048]{1,0:T(8,128)S(1)} %reshape.130, f32[320]{0:T(512)S(1)} %reshape.131), kind=kOutput, calls=%fused_computation.7 | convolution fusion | flops 1009516544 | bytes 6259968 | tf_op jit(solution)/shard_map/dot_general | solution.py:66
  172.6 3.3 %multiply_convert_fusion = bf16[32,10,2048]{2,1,0:T(8,128)(2,1)} fusion(f32[32,10]{1,0:T(8,128)S(1)} %bitcast.54, bf16[32,10,2048]{2,1,0:T(8,128)(2,1)} %all-to-all-done.1), kind=kLoop, calls=%fused_computation.6 | loop fusion | flops 1966080 | bytes 2622720 | tf_op jit(solution)/shard_map/convert_element_type | solution.py:40
  175.9 3.6 %convert_element_type.80 = bf16[320,2048]{1,0:T(8,128)(2,1)} reshape(bf16[32,10,2048]{2,1,0:T(8,128)(2,1)} %multiply_convert_fusion) | data formatting | bytes 2621440 | tf_op jit(solution)/shard_map/convert_element_type | solution.py:40
  179.5 59.1 %all-gather.4.cloned.1.call-done = bf16[1,2048,768]{2,1,0:T(8,128)(2,1)} async-done(((bf16[1,128,768]{2,1,0:T(8,128)(2,1)}), bf16[1,2048,768]{2,1,0:T(8,128)(2,1)}) %all-gather.4.cloned.1.call-update) | async-done | bytes 3145744 | tf_op jit(solution)/shard_map/all_gather | solution.py:52
  238.7 3.2 fusion.21
  241.9 0.7 convert_element_type.96
  242.6 7.4 %all-to-all-start.4 = ((bf16[32,1,10]{2,1,0:T(2,128)(2,1)}), bf16[32,1,10]{2,1,0:T(2,128)(2,1)S(1)}, u32[]{:S(2)}, u32[]{:S(2)}) async-start(bf16[32,1,10]{2,1,0:T(2,128)(2,1)} %convert_element_type.96), calls=%async_computation.4 | async-start | bytes 32768 | tf_op jit(solution)/shard_map/all_to_all | solution.py:82
  250.1 3.6 %fusion.10 = f32[320,768]{1,0:T(8,128)S(1)} fusion(bf16[320,2048]{1,0:T(8,128)(2,1)} %convert_element_type.80, bf16[1,2048,768]{2,1,0:T(8,128)(2,1)} %all-gather.4.cloned.1.call-done), kind=kOutput, calls=%fused_computation.18 | convolution fusion | flops 1006632960 | bytes 5439488 | tf_op jit(solution)/shard_map/dot_general | solution.py:54
  253.8 1.3 fusion
  255.2 0.7 copy-done.3
  255.8 1.2 fusion.18
  257.0 1.6 reshape.125
  258.6 7.4 %all-to-all-start.3 = ((bf16[32,10,2048]{2,1,0:T(8,128)(2,1)}), bf16[32,10,2048]{2,1,0:T(8,128)(2,1)S(1)}, u32[]{:S(2)}, u32[]{:S(2)}) async-start(bf16[32,10,2048]{2,1,0:T(8,128)(2,1)} %reshape.125), calls=%async_computation.3 | async-start | bytes 4194304 | tf_op jit(solution)/shard_map/all_to_all | solution.py:75
  266.2 1.9 gather_fusion.4
  268.3 0.6 copy.23
  268.9 23.0 %all-to-all-done.3 = bf16[32,10,2048]{2,1,0:T(8,128)(2,1)S(1)} async-done(((bf16[32,10,2048]{2,1,0:T(8,128)(2,1)}), bf16[32,10,2048]{2,1,0:T(8,128)(2,1)S(1)}, u32[]{:S(2)}, u32[]{:S(2)}) %all-to-all-start.3) | async-done | bytes 1310752 | tf_op jit(solution)/shard_map/all_to_all | solution.py:75
  291.9 0.5 reshape.126
  292.4 1.4 gather_fusion.3
  293.8 0.7 gather.21
  294.5 3.6 %reduce_sum.34 = bf16[128,2048]{1,0:T(8,128)(2,1)} reduce(bf16[128,2,2048]{2,1,0:T(2,128)(2,1)S(1)} %gather.21, bf16[]{:T(256)} %constant.36.clone.1), dimensions={1}, to_apply=%region_4.5 | reduce | flops 262144 | bytes 1572866 | tf_op jit(solution)/shard_map/reduce_sum | solution.py:93
  298.1 17.8 %reduce-scatter.2.cloned.1.call-done = bf16[128,768]{1,0:T(8,128)(2,1)} async-done(((bf16[2048,768]{1,0:T(8,128)(2,1)}), bf16[128,768]{1,0:T(8,128)(2,1)}) %reduce-scatter.2.cloned.1.call-update) | async-done | bytes 196624 | tf_op jit(solution)/shard_map/reduce_scatter | solution.py:65
  (41 shorter events, 1.9 us)
Async XLA Ops:
  7.2 20.3 %copy-start = (bf16[128,2048]{1,0:T(8,128)(2,1)S(1)}, bf16[128,2048]{1,0:T(8,128)(2,1)}, u32[]{:S(2)}) copy-start(bf16[128,2048]{1,0:T(8,128)(2,1)} %param.7) | copy-start | bytes 1572868
  7.2 94.0 %all-gather.8.cloned.1.call-start = ((), (), s32[]{:S(2)}) async-start(), calls=%async_computation.8 | async-start | bytes 3342336 | tf_op jit(solution)/shard_map/all_gather | solution.py:42
  7.9 156.4 %all-gather.6.cloned.1.call-start = ((), (), s32[]{:S(2)}) async-start(), calls=%async_computation.7 | async-start | bytes 3342336 | tf_op jit(solution)/shard_map/all_gather | solution.py:43
  8.7 230.0 %all-gather.4.cloned.1.call-start = ((), (), s32[]{:S(2)}) async-start(), calls=%async_computation.6 | async-start | bytes 3342336 | tf_op jit(solution)/shard_map/all_gather | solution.py:52
  18.0 14.7 %all-to-all-start = ((bf16[32,1,10]{2,1,0:T(2,128)(2,1)}), bf16[32,1,10]{2,1,0:T(2,128)(2,1)S(1)}, u32[]{:S(2)}, u32[]{:S(2)}) async-start(bf16[32,1,10]{2,1,0:T(2,128)(2,1)} %all_to_all.25), calls=%async_computation | async-start | bytes 32768 | tf_op jit(solution)/shard_map/all_to_all | solution.py:35
  31.6 7.5 %copy-start.1 = (bf16[128,2048]{1,0:T(8,128)(2,1)S(1)}, bf16[128,2048]{1,0:T(8,128)(2,1)}, u32[]{:S(2)}) copy-start(bf16[128,2048]{1,0:T(8,128)(2,1)} %param.8) | copy-start | bytes 1572868
  32.7 32.4 %all-to-all-start.2 = ((bf16[32,10,2048]{2,1,0:T(8,128)(2,1)}), bf16[32,10,2048]{2,1,0:T(8,128)(2,1)S(1)}, u32[]{:S(2)}, u32[]{:S(2)}) async-start(bf16[32,10,2048]{2,1,0:T(8,128)(2,1)} %reshape.123), calls=%async_computation.2 | async-start | bytes 4194304 | tf_op jit(solution)/shard_map/all_to_all | solution.py:33
  65.0 33.6 %all-to-all-start.1 = ((bf16[32,10,2048]{2,1,0:T(8,128)(2,1)}), bf16[32,10,2048]{2,1,0:T(8,128)(2,1)}, u32[]{:S(2)}, u32[]{:S(2)}) async-start(bf16[32,10,2048]{2,1,0:T(8,128)(2,1)} %reshape.122), calls=%async_computation.1 | async-start | bytes 4194304 | tf_op jit(solution)/shard_map/all_to_all | solution.py:34
  72.7 243.2 %reduce-scatter.2.cloned.1.call-start = ((), (), s32[]{:S(2)}) async-start(), calls=%async_computation.9 | async-start | bytes 3342336 | tf_op jit(solution)/shard_map/reduce_scatter | solution.py:65
  242.6 16.0 %all-to-all-start.4 = ((bf16[32,1,10]{2,1,0:T(2,128)(2,1)}), bf16[32,1,10]{2,1,0:T(2,128)(2,1)S(1)}, u32[]{:S(2)}, u32[]{:S(2)}) async-start(bf16[32,1,10]{2,1,0:T(2,128)(2,1)} %convert_element_type.96), calls=%async_computation.4 | async-start | bytes 32768 | tf_op jit(solution)/shard_map/all_to_all | solution.py:82
  250.0 3.6 %copy-start.2 = (bf16[1,2048,768]{2,1,0:T(8,128)(2,1)S(1)}, bf16[1,2048,768]{2,1,0:T(8,128)(2,1)}, u32[]{:S(2)}) copy-start(bf16[1,2048,768]{2,1,0:T(8,128)(2,1)} %all-gather.8.cloned.1.call-done) | copy-start | bytes 9437188
  250.0 3.6 %copy-start.4 = (f32[320,768]{1,0:T(8,128)S(1)}, f32[320,768]{1,0:T(8,128)}, u32[]{:S(2)}) copy-start(f32[320,768]{1,0:T(8,128)} %fusion.2) | copy-start | bytes 2949124
  250.0 3.8 %copy-start.5 = (f32[320,768]{1,0:T(8,128)S(1)}, f32[320,768]{1,0:T(8,128)}, u32[]{:S(2)}) copy-start(f32[320,768]{1,0:T(8,128)} %get-tuple-element.12) | copy-start | bytes 2949124
  253.8 2.0 copy-start.3
  258.6 33.3 %all-to-all-start.3 = ((bf16[32,10,2048]{2,1,0:T(8,128)(2,1)}), bf16[32,10,2048]{2,1,0:T(8,128)(2,1)S(1)}, u32[]{:S(2)}, u32[]{:S(2)}) async-start(bf16[32,10,2048]{2,1,0:T(8,128)(2,1)} %reshape.125), calls=%async_computation.3 | async-start | bytes 4194304 | tf_op jit(solution)/shard_map/all_to_all | solution.py:75
Sparse Core Ops, SparseCore 0:
  10.1 79.8 all-gather.7
  92.0 72.2 all-gather.5
  166.4 72.2 all-gather.3
  241.9 73.9 reduce-scatter.1
where the time goes:
time: 323 us; the launch traced here: 322 us
  waiting for transfers between devices  205 us (63%)
  starting transfers between devices  38.7 us (12%)
  local copies, waits for them, and re-layouts  32.9 us (10%)
  matrix products  22.1 us (7%)
  between operations  14.1 us (4%)
  other arithmetic  9.22 us (3%)
    all_gather x1, waiting for transfers between devices, per_device(): piece_rows = lax.all_gather(w_down, 'dp', axis=1, tiled=True)[0]  59.1 us
    all_gather x1, waiting for transfers between devices, per_device(): lax.all_gather(w_up, 'dp', axis=1, tiled=True)  58.7 us
    all_to_all x1, waiting for transfers between devices, per_device(): lax.all_to_all(dy_slots, 'expert', split_axis=0, concat_axis=0, tiled=True)  24.1 us
    all_to_all x1, waiting for transfers between devices, per_device(): lax.all_to_all(x_grad.reshape(n_expert, capacity, model_width), 'expert',...  23 us
    all_to_all x1, waiting for transfers between devices, per_device(): lax.all_to_all(x_slots, 'expert', split_axis=0, concat_axis=0, tiled=True)  19.5 us
    reduce_scatter x1, waiting for transfers between devices, per_device(): lax.psum_scatter(lax.dot_general(scaled, hidden, (((0,), (0,)), ((), ()))...  17.8 us
    all_to_all x1, starting transfers between devices, per_device(): lax.all_to_all(p_slots, 'expert', split_axis=0, concat_axis=0, tiled=True)  9.43 us
    all_to_all x1, starting transfers between devices, per_device(): lax.all_to_all(dy_slots, 'expert', split_axis=0, concat_axis=0, tiled=True)  7.69 us
  transfers between devices with their start and end apart: 9, of which 7 were waited for; matrix products, arithmetic and copies ran while one was open for 19% of the time, Pallas kernels for 0%

commit v1 on v0

--- a/solution.py
+++ b/solution.py
@@ -1,7 +1,18 @@
+import functools
 import jax
 import jax.numpy as jnp
 from jax import lax
 from jax.sharding import PartitionSpec as P
+
+
+def keep_up_points(message, group_axis):
+    vec_out = jnp.stack([message for _ in range(lax.axis_size(group_axis))], axis=0)
+    shaped = lax.all_to_all(vec_out, group_axis, 0, 0)
+    piece_next = jnp.concatenate(shaped, axis=1)
+    return piece_next
+
+
+attach_knots_in = functools.partial(keep_up_points, group_axis="dp")
 
 
 def per_device(x_tokens, grad_out, expert_ids, route_probs, w_gate, w_up, w_down):
@@ -49,7 +60,7 @@
     gate_sig = jax.nn.sigmoid(gate_pre)
     gate_act = gate_pre * gate_sig
     hidden = (gate_act * up_pre).astype(jnp.bfloat16)
-    piece_rows = lax.all_gather(w_down, "dp", axis=1, tiled=True)[0]
+    piece_rows = attach_knots_in(w_down)[0]
     out_piece = jnp.dot(hidden, piece_rows.T, preferred_element_type=jnp.float32)
     grad_sum = jnp.dot(scaled, piece_rows, preferred_element_type=jnp.float32)
     prob_sum = jnp.sum(dy_rows.astype(jnp.float32) * out_piece, axis=1)

time: 323 us -> 380 us (1.18)
  the two profiles are of different devices: /device:TPU:4 before, /device:TPU:2 now
where the time goes in v1:
time: 380 us; the launch traced here: 379 us
  waiting for transfers between devices  223 us (59%)
  starting transfers between devices  42 us (11%)
  local copies, waits for them, and re-layouts  35.8 us (9%)
  blocking collectives  33.4 us (9%)
  matrix products  22.1 us (6%)
  between operations  14 us (4%)
  other arithmetic  9.21 us (2%)
    all_gather x1, waiting for transfers between devices, per_device(): lax.all_gather(w_up, 'dp', axis=1, tiled=True)  169 us
    all_to_all x1, blocking collectives, per_device(): lax.all_to_all(dy_slots, 'expert', split_axis=0, concat_axis=0, tiled=True)  33.4 us
    all_to_all x1, waiting for transfers between devices, per_device(): lax.all_to_all(x_grad.reshape(n_expert, capacity, model_width), 'expert',...  23 us
    all_to_all x1, waiting for transfers between devices, per_device(): lax.all_to_all(x_slots, 'expert', split_axis=0, concat_axis=0, tiled=True)  19.5 us
    all_to_all x1, starting transfers between devices, keep_up_points(): shaped = lax.all_to_all(vec_out, group_axis, 0, 0)  13.4 us
    all_to_all x1, starting transfers between devices, per_device(): lax.all_to_all(p_slots, 'expert', split_axis=0, concat_axis=0, tiled=True)  9.41 us
    reduce_scatter x1, waiting for transfers between devices, per_device(): lax.psum_scatter(lax.dot_general(scaled, hidden, (((0,), (0,)), ((), ()))...  8.8 us
  transfers between devices with their start and end apart: 8, of which 5 were waited for; matrix products, arithmetic and copies ran while one was open for 17% of the time, Pallas kernels for 0%

profile of v1, /device:TPU:2, one launch (start us, length us, event | category | flops | bytes accessed | tf_op | source)
XLA Modules:
  0.0 379.4 jit_solution(1607836383480812416)
XLA Ops:
  7.2 0.7 all-gather.5.cloned.1.call-update
  7.9 0.8 copy.18
  9.0 0.7 broadcast_multiply_fusion
  9.9 0.6 reduce-window.6
  10.5 0.2 slice_reduce_fusion
  10.7 0.7 convert.9
  11.8 1.4 scatter_custom_fusion
  13.3 2.5 gather_fusion
  15.8 0.7 all_to_all.29
  16.5 9.4 %all-to-all-start = ((bf16[32,1,10]{2,1,0:T(2,128)(2,1)}), bf16[32,1,10]{2,1,0:T(2,128)(2,1)S(1)}, u32[]{:S(2)}, u32[]{:S(2)}) async-start(bf16[32,1,10]{2,1,0:T(2,128)(2,1)} %all_to_all.29), calls=%async_computation | async-start | bytes 32768 | tf_op jit(solution)/shard_map/all_to_all | solution.py:46
  25.9 1.1 concatenate.12
  27.0 2.4 gather_fusion.2
  29.4 1.6 reshape.126
  31.0 1.1 all-to-all-done
  32.1 6.5 %all-to-all-start.3 = ((bf16[32,10,2048]{2,1,0:T(8,128)(2,1)}), bf16[32,10,2048]{2,1,0:T(8,128)(2,1)S(1)}, u32[]{:S(2)}, u32[]{:S(2)}) async-start(bf16[32,10,2048]{2,1,0:T(8,128)(2,1)} %reshape.126), calls=%async_computation.3 | async-start | bytes 4194304 | tf_op jit(solution)/shard_map/all_to_all | solution.py:44
  38.7 3.0 gather_fusion.1
  41.7 3.4 reshape.125
  45.1 19.5 %all-to-all-done.3 = bf16[32,10,2048]{2,1,0:T(8,128)(2,1)S(1)} async-done(((bf16[32,10,2048]{2,1,0:T(8,128)(2,1)}), bf16[32,10,2048]{2,1,0:T(8,128)(2,1)S(1)}, u32[]{:S(2)}, u32[]{:S(2)}) %all-to-all-start.3) | async-done | bytes 1310752 | tf_op jit(solution)/shard_map/all_to_all | solution.py:44
  64.5 33.4 %all_to_all.36 = bf16[32,10,2048]{2,1,0:T(8,128)(2,1)} all-to-all(bf16[32,10,2048]{2,1,0:T(8,128)(2,1)} %reshape.125), channel_id=1, replica_groups=mesh['dp'=16,'expert'=32] {'expert'}, dimensions={0} | all-to-all | bytes 2621440 | tf_op jit(solution)/shard_map/all_to_all | solution.py:45
  98.0 2.0 stack.2
  99.9 13.4 %all-to-all-start.2 = ((bf16[16,1,128,768]{3,2,1,0:T(8,128)(2,1)}), bf16[16,1,128,768]{3,2,1,0:T(8,128)(2,1)}, u32[]{:S(2)}, u32[]{:S(2)}) async-start(bf16[16,1,128,768]{3,2,1,0:T(8,128)(2,1)} %stack.2), calls=%async_computation.2 | async-start | bytes 6291456 | tf_op jit(solution)/shard_map/all_to_all | solution.py:10
  113.4 0.7 all-gather.3.cloned.1.call-update
  114.1 0.2 reduce-scatter.2.cloned.1.call-start
  114.5 1.3 reshape.127
  115.8 2.5 reshape.133
  118.3 4.4 %fusion.2 = f32[320,768]{1,0:T(8,128)} fusion(bf16[320,2048]{1,0:T(8,128)(2,1)} %reshape.127, bf16[1,2048,768]{2,1,0:T(8,128)(2,1)} %all-gather.5.cloned.1.call-done), kind=kOutput, calls=%fused_computation.10 | convolution fusion | flops 1006632960 | bytes 5439488 | tf_op jit(solution)/shard_map/dot_general | solution.py:58
  122.7 169.0 %all-gather.3.cloned.1.call-done = bf16[1,2048,768]{2,1,0:T(8,128)(2,1)} async-done(((bf16[1,128,768]{2,1,0:T(8,128)(2,1)}), bf16[1,2048,768]{2,1,0:T(8,128)(2,1)}) %all-gather.3.cloned.1.call-update) | async-done | bytes 3145744 | tf_op jit(solution)/shard_map/all_gather | solution.py:54
  291.7 4.7 %multiply_convert_fusion.3 = (bf16[320,768]{1,0:T(8,128)(2,1)S(1)}, f32[320,768]{1,0:T(8,128)}) fusion(f32[320,768]{1,0:T(8,128)} %fusion.2, bf16[320,2048]{1,0:T(8,128)(2,1)} %reshape.127, bf16[1,2048,768]{2,1,0:T(8,128)(2,1)} %all-gather.3.cloned.1.call-done), kind=kOutput, calls=%fused_computation.22 | convolution fusion | flops 1008107520 | bytes 6914048 | tf_op jit(solution)/shard_map/dot_general | solution.py:59
  296.4 3.6 convolution_convert_fusion
  300.1 3.3 multiply_convert_fusion
  303.4 3.6 convert_element_type.80
  307.0 3.2 fusion.14
  310.2 0.7 convert_element_type.96
  311.0 5.0 %all-to-all-start.5 = ((bf16[32,1,10]{2,1,0:T(2,128)(2,1)}), bf16[32,1,10]{2,1,0:T(2,128)(2,1)S(1)}, u32[]{:S(2)}, u32[]{:S(2)}) async-start(bf16[32,1,10]{2,1,0:T(2,128)(2,1)} %convert_element_type.96), calls=%async_computation.5 | async-start | bytes 32768 | tf_op jit(solution)/shard_map/all_to_all | solution.py:93
  316.0 3.6 fusion.30
  319.8 1.3 fusion
  321.2 0.5 copy-done.3
  321.7 1.2 fusion.11
  322.9 1.6 reshape.128
  324.5 7.4 %all-to-all-start.4 = ((bf16[32,10,2048]{2,1,0:T(8,128)(2,1)}), bf16[32,10,2048]{2,1,0:T(8,128)(2,1)S(1)}, u32[]{:S(2)}, u32[]{:S(2)}) async-start(bf16[32,10,2048]{2,1,0:T(8,128)(2,1)} %reshape.128), calls=%async_computation.4 | async-start | bytes 4194304 | tf_op jit(solution)/shard_map/all_to_all | solution.py:86
  332.1 1.9 gather_fusion.4
  334.2 0.6 copy.23
  334.8 23.0 %all-to-all-done.4 = bf16[32,10,2048]{2,1,0:T(8,128)(2,1)S(1)} async-done(((bf16[32,10,2048]{2,1,0:T(8,128)(2,1)}), bf16[32,10,2048]{2,1,0:T(8,128)(2,1)S(1)}, u32[]{:S(2)}, u32[]{:S(2)}) %all-to-all-start.4) | async-done | bytes 1310752 | tf_op jit(solution)/shard_map/all_to_all | solution.py:86
  357.8 0.5 reshape.129
  358.3 1.4 gather_fusion.3
  359.7 0.7 gather.21
  360.4 3.6 reduce_sum.34
  364.0 8.8 %reduce-scatter.2.cloned.1.call-done = bf16[128,768]{1,0:T(8,128)(2,1)} async-done(((bf16[2048,768]{1,0:T(8,128)(2,1)}), bf16[128,768]{1,0:T(8,128)(2,1)}) %reduce-scatter.2.cloned.1.call-update) | async-done | bytes 196624 | tf_op jit(solution)/shard_map/reduce_scatter | solution.py:76
  (40 shorter events, 1.8 us)
Async XLA Ops:
  7.2 111.2 %all-gather.5.cloned.1.call-start = ((), (), s32[]{:S(2)}) async-start(), calls=%async_computation.8 | async-start | bytes 3342336 | tf_op jit(solution)/shard_map/all_gather | solution.py:53
  16.5 15.6 %all-to-all-start = ((bf16[32,1,10]{2,1,0:T(2,128)(2,1)}), bf16[32,1,10]{2,1,0:T(2,128)(2,1)S(1)}, u32[]{:S(2)}, u32[]{:S(2)}) async-start(bf16[32,1,10]{2,1,0:T(2,128)(2,1)} %all_to_all.29), calls=%async_computation | async-start | bytes 32768 | tf_op jit(solution)/shard_map/all_to_all | solution.py:46
  31.0 7.6 %copy-start = (bf16[128,2048]{1,0:T(8,128)(2,1)S(1)}, bf16[128,2048]{1,0:T(8,128)(2,1)}, u32[]{:S(2)}) copy-start(bf16[128,2048]{1,0:T(8,128)(2,1)} %param.8) | copy-start | bytes 1572868
  32.1 32.4 %all-to-all-start.3 = ((bf16[32,10,2048]{2,1,0:T(8,128)(2,1)}), bf16[32,10,2048]{2,1,0:T(8,128)(2,1)S(1)}, u32[]{:S(2)}, u32[]{:S(2)}) async-start(bf16[32,10,2048]{2,1,0:T(8,128)(2,1)} %reshape.126), calls=%async_computation.3 | async-start | bytes 4194304 | tf_op jit(solution)/shard_map/all_to_all | solution.py:44
  45.1 52.9 %copy-start.1 = (bf16[1,128,768]{2,1,0:T(8,128)(2,1)S(1)}, bf16[1,128,768]{2,1,0:T(8,128)(2,1)}, u32[]{:S(2)}) copy-start(bf16[1,128,768]{2,1,0:T(8,128)(2,1)} %param.13) | copy-start | bytes 589828
  99.9 207.1 %all-to-all-start.2 = ((bf16[16,1,128,768]{3,2,1,0:T(8,128)(2,1)}), bf16[16,1,128,768]{3,2,1,0:T(8,128)(2,1)}, u32[]{:S(2)}, u32[]{:S(2)}) async-start(bf16[16,1,128,768]{3,2,1,0:T(8,128)(2,1)} %stack.2), calls=%async_computation.2 | async-start | bytes 6291456 | tf_op jit(solution)/shard_map/all_to_all | solution.py:10
  113.3 178.4 %all-gather.3.cloned.1.call-start = ((), (), s32[]{:S(2)}) async-start(), calls=%async_computation.7 | async-start | bytes 3342336 | tf_op jit(solution)/shard_map/all_gather | solution.py:54
  114.1 258.8 %reduce-scatter.2.cloned.1.call-start = ((), (), s32[]{:S(2)}) async-start(), calls=%async_computation.9 | async-start | bytes 3342336 | tf_op jit(solution)/shard_map/reduce_scatter | solution.py:76
  311.0 13.6 %all-to-all-start.5 = ((bf16[32,1,10]{2,1,0:T(2,128)(2,1)}), bf16[32,1,10]{2,1,0:T(2,128)(2,1)S(1)}, u32[]{:S(2)}, u32[]{:S(2)}) async-start(bf16[32,1,10]{2,1,0:T(2,128)(2,1)} %convert_element_type.96), calls=%async_computation.5 | async-start | bytes 32768 | tf_op jit(solution)/shard_map/all_to_all | solution.py:93
  316.0 3.6 copy-start.2
  316.0 3.6 copy-start.4
  316.0 3.8 %copy-start.5 = (f32[320,768]{1,0:T(8,128)S(1)}, f32[320,768]{1,0:T(8,128)}, u32[]{:S(2)}) copy-start(f32[320,768]{1,0:T(8,128)} %get-tuple-element.12) | copy-start | bytes 2949124
  319.8 1.9 copy-start.3
  324.5 33.3 %all-to-all-start.4 = ((bf16[32,10,2048]{2,1,0:T(8,128)(2,1)}), bf16[32,10,2048]{2,1,0:T(8,128)(2,1)S(1)}, u32[]{:S(2)}, u32[]{:S(2)}) async-start(bf16[32,10,2048]{2,1,0:T(8,128)(2,1)} %reshape.128), calls=%async_computation.4 | async-start | bytes 4194304 | tf_op jit(solution)/shard_map/all_to_all | solution.py:86
Sparse Core Ops, SparseCore 0:
  10.1 79.8 all-gather.4
  116.2 175.4 all-gather.2
  300.2 72.5 reduce-scatter.1
